TPU v7x, 512 devices: a whole 4x4x16 slice. The times are simulated.
512 devices in a mesh: expert: 128 (over x, z, core), dp: 4 (over y).
Axes of the slice: x: 4, y: 4, z: 16, core: 2. Of those that a mesh axis runs over, the one named last changes fastest.
Arguments:
- tokens: bfloat16 [16384, 3584], P('expert', 'dp'), may hold values from -6 to 6
- route_ids: int32 [16384, 8], P('expert'), may hold values from 0 to 127, as said below
- gate_scores: float32 [16384, 8], P('expert'), may hold values from 0.1 to 1, as said below
- up_weight: bfloat16 [128, 3584, 1024], P('expert', 'dp'), may hold values from -0.09375 to 0.09375
- down_weight: bfloat16 [128, 1024, 3584], P('expert', None, 'dp'), may hold values from -0.1875 to 0.1875
Outputs:
- mixed: bfloat16 [16384, 3584], P('expert', 'dp')
Inputs may be any that keep to these rules, and one draw needn't show every extreme that they name: `route_ids`: each row names 8 different experts. The same 2 experts are named by exactly 15 rows in every aligned block of 128 rows (the tokens of one device); in such a block every other expert is named by 8 - 1 or 8 rows. `gate_scores`: positive affinities.
All inputs are finite; a program needn't handle non-finite values.
Results may differ from a plain program's by a relative error of at most 0.017.
Values may be sent and summed in bfloat16 or wider, within the bound.
No kernel may reach another device: no remote copies, remote signals or barrier semaphores. Data moves between devices by JAX's collectives and lax.ppermute only.
A program may use at most 64 MiB of HBM per device.

v0:
```python
import jax
import jax.numpy as jnp
from jax import lax
from jax.sharding import PartitionSpec as P

HOT = 2
CHUNKS = 3
ROUTE_SCALE = 2.5


def silu_hidden(before):
    summed = lax.psum(before.astype(jnp.bfloat16), "dp").astype(jnp.float32)
    result = jax.nn.silu(summed).astype(jnp.bfloat16)
    return result


def expert_chunk(piece, up_local, down_local, previous):
    experts, item_count, features = piece.shape
    arrived = lax.all_to_all(piece, "expert", split_axis=0, concat_axis=0, tiled=True)
    flat_rows = arrived.reshape(-1, features)
    before = jnp.dot(flat_rows, up_local, preferred_element_type=jnp.float32)
    if previous is not None:
        before, previous = lax.optimization_barrier((before, previous))
    hidden = silu_hidden(before)
    output = jnp.dot(hidden, down_local, preferred_element_type=jnp.float32)
    outcome = output.astype(jnp.bfloat16).reshape(experts, item_count, features)
    returned = lax.all_to_all(outcome, "expert", split_axis=0, concat_axis=0, tiled=True)
    return (returned, hidden)


def local(tokens, route_ids, gate_scores, up_weight, down_weight):
    token_count, chosen_count = route_ids.shape
    features = tokens.shape[1]
    experts = lax.axis_size("expert")
    mean_rows = token_count * chosen_count // experts
    hot_most = min(2 * mean_rows - 1, token_count)
    cold_rows = (experts - HOT) * mean_rows - HOT * (hot_most - mean_rows)
    cold_most = -(-cold_rows // (experts - HOT))
    flat_ids = route_ids.reshape(-1)
    row_total = flat_ids.shape[0]
    expert_range = jnp.arange(experts, dtype=jnp.int32)
    onehot = (flat_ids[:, None] == expert_range[None, :]).astype(jnp.int32)
    running = jnp.cumsum(onehot, axis=0) - 1
    row_ranks = jnp.sum(onehot * running, axis=1)
    padded = jnp.concatenate([tokens, jnp.zeros((1, features), tokens.dtype)], axis=0)
    up_local = up_weight[0]
    down_local = down_weight[0]
    mix_weights = gate_scores * (ROUTE_SCALE / jnp.sum(gate_scores, axis=1, keepdims=True))
    slot_count = max(hot_most, cold_most)
    slot_of_row = flat_ids * slot_count + row_ranks
    slot_table = jnp.full((experts * slot_count,), row_total, jnp.int32)
    slot_table = slot_table.at[slot_of_row].set(jnp.arange(row_total, dtype=jnp.int32), mode="drop")
    sending = padded[slot_table // chosen_count].reshape(experts, slot_count, features)
    bounds = [slot_count * c // CHUNKS for c in range(CHUNKS + 1)]
    pieces = []
    previous = None
    for lo, hi in zip(bounds[:-1], bounds[1:]):
        returned, previous = expert_chunk(sending[:, lo:hi], up_local, down_local, previous)
        pieces.append(returned)
    returned = jnp.concatenate(pieces, axis=1).reshape(-1, features)
    picked = returned[slot_of_row]
    picked = picked.reshape(token_count, chosen_count, features).astype(jnp.float32)
    mixed = jnp.sum(mix_weights[:, :, None] * picked, axis=1)
    return mixed.astype(jnp.bfloat16)


def solution(mesh):
    return jax.shard_map(
        local,
        mesh=mesh,
        in_specs=(
            P("expert", "dp"),
            P("expert", None),
            P("expert", None),
            P("expert", "dp", None),
            P("expert", None, "dp"),
        ),
        out_specs=P("expert", "dp"),
        check_vma=False,
    )
```

profile of v0, /device:TPU:1, one launch (start us, length us, event | category | flops | bytes accessed | tf_op | source)
XLA Modules:
  0.0 652.5 jit_solution(6864148417399794794)
XLA Ops:
  9.4 4.3 scatter_custom_fusion
  13.8 7.1 %gather_fusion = bf16[1920,896]{1,0:T(8,128)(2,1)} fusion(bf16[129,896]{1,0:T(8,128)(2,1)S(1)} %concatenate.6, s32[2048]{0:T(1024)S(1)} %pad_clamp_fusion), kind=kCustom, calls=%fused_computation | custom fusion | bytes 6888960 | tf_op jit(solution)/shard_map/gather | solution.py:53
  21.0 5.7 reshape.81
  26.7 5.4 fusion.48
  32.1 108.1 %all_to_all.30 = bf16[128,5,896]{2,1,0:T(8,128)(2,1)} all-to-all(bf16[128,5,896]{2,1,0:T(8,128)(2,1)S(1)} %get-tuple-element.9), channel_id=1, replica_groups=mesh['expert'=128,'dp'=4] {'expert'}, dimensions={0} | all-to-all | bytes 2293760 | tf_op jit(solution)/shard_map/all_to_all | solution.py:19
  140.2 96.5 %all_to_all.31 = bf16[128,5,896]{2,1,0:T(8,128)(2,1)} all-to-all(bf16[128,5,896]{2,1,0:T(8,128)(2,1)S(1)} %get-tuple-element.11), channel_id=1, replica_groups=mesh['expert'=128,'dp'=4] {'expert'}, dimensions={0} | all-to-all | bytes 2293760 | tf_op jit(solution)/shard_map/all_to_all | solution.py:19
  236.7 9.1 %all-to-all-start.4 = ((bf16[128,5,896]{2,1,0:T(8,128)(2,1)}), bf16[128,5,896]{2,1,0:T(8,128)(2,1)}, u32[]{:S(2)}, u32[]{:S(2)}) async-start(bf16[128,5,896]{2,1,0:T(8,128)(2,1)} %get-tuple-element.10), calls=%async_computation.4 | async-start | bytes 3670016 | tf_op jit(solution)/shard_map/all_to_all | solution.py:19
  251.2 63.4 %all-reduce.5.cloned.1.call-done = bf16[640,1024]{1,0:T(8,128)(2,1)} async-done(((bf16[640,1024]{1,0:T(8,128)(2,1)}), bf16[640,1024]{1,0:T(8,128)(2,1)}) %all-reduce.5.cloned.1.call-update) | async-done | bytes 1310736 | tf_op jit(solution)/shard_map/psum | solution.py:12
  319.8 13.6 %all-to-all-done.4 = bf16[128,5,896]{2,1,0:T(8,128)(2,1)} async-done(((bf16[128,5,896]{2,1,0:T(8,128)(2,1)}), bf16[128,5,896]{2,1,0:T(8,128)(2,1)}, u32[]{:S(2)}, u32[]{:S(2)}) %all-to-all-start.4) | async-done | bytes 1146912 | tf_op jit(solution)/shard_map/all_to_all | solution.py:19
  333.4 9.1 %all-to-all-start.1 = ((bf16[128,5,896]{2,1,0:T(8,128)(2,1)}), bf16[128,5,896]{2,1,0:T(8,128)(2,1)}, u32[]{:S(2)}, u32[]{:S(2)}) async-start(bf16[128,5,896]{2,1,0:T(8,128)(2,1)} %reshape.83), calls=%async_computation.1 | async-start | bytes 3670016 | tf_op jit(solution)/shard_map/all_to_all | solution.py:27
  345.1 2.6 fusion.21
  347.7 63.4 %all-reduce.7.cloned.1.call-done = bf16[640,1024]{1,0:T(8,128)(2,1)} async-done(((bf16[640,1024]{1,0:T(8,128)(2,1)}), bf16[640,1024]{1,0:T(8,128)(2,1)}) %all-reduce.7.cloned.1.call-update) | async-done | bytes 1310736 | tf_op jit(solution)/shard_map/psum | solution.py:12
  416.3 13.8 %all-to-all-done.1 = bf16[128,5,896]{2,1,0:T(8,128)(2,1)} async-done(((bf16[128,5,896]{2,1,0:T(8,128)(2,1)}), bf16[128,5,896]{2,1,0:T(8,128)(2,1)}, u32[]{:S(2)}, u32[]{:S(2)}) %all-to-all-start.1) | async-done | bytes 1146912 | tf_op jit(solution)/shard_map/all_to_all | solution.py:27
  430.1 9.1 %all-to-all-start.3 = ((bf16[128,5,896]{2,1,0:T(8,128)(2,1)}), bf16[128,5,896]{2,1,0:T(8,128)(2,1)}, u32[]{:S(2)}, u32[]{:S(2)}) async-start(bf16[128,5,896]{2,1,0:T(8,128)(2,1)} %reshape.85), calls=%async_computation.3 | async-start | bytes 3670016 | tf_op jit(solution)/shard_map/all_to_all | solution.py:27
  442.0 2.6 fusion.19
  444.6 63.4 %all-reduce.9.cloned.1.call-done = bf16[640,1024]{1,0:T(8,128)(2,1)} async-done(((bf16[640,1024]{1,0:T(8,128)(2,1)}), bf16[640,1024]{1,0:T(8,128)(2,1)}) %all-reduce.9.cloned.1.call-update) | async-done | bytes 1310736 | tf_op jit(solution)/shard_map/psum | solution.py:12
  508.0 3.4 fusion.34
  513.0 13.8 %all-to-all-done.3 = bf16[128,5,896]{2,1,0:T(8,128)(2,1)} async-done(((bf16[128,5,896]{2,1,0:T(8,128)(2,1)}), bf16[128,5,896]{2,1,0:T(8,128)(2,1)}, u32[]{:S(2)}, u32[]{:S(2)}) %all-to-all-start.3) | async-done | bytes 1146912 | tf_op jit(solution)/shard_map/all_to_all | solution.py:27
  526.8 9.1 %all-to-all-start.5 = ((bf16[128,5,896]{2,1,0:T(8,128)(2,1)}), bf16[128,5,896]{2,1,0:T(8,128)(2,1)}, u32[]{:S(2)}, u32[]{:S(2)}) async-start(bf16[128,5,896]{2,1,0:T(8,128)(2,1)} %reshape.87), calls=%async_computation.5 | async-start | bytes 3670016 | tf_op jit(solution)/shard_map/all_to_all | solution.py:27
  536.1 87.4 %all-to-all-done.5 = bf16[128,5,896]{2,1,0:T(8,128)(2,1)} async-done(((bf16[128,5,896]{2,1,0:T(8,128)(2,1)}), bf16[128,5,896]{2,1,0:T(8,128)(2,1)}, u32[]{:S(2)}, u32[]{:S(2)}) %all-to-all-start.5) | async-done | bytes 1146912 | tf_op jit(solution)/shard_map/all_to_all | solution.py:27
  623.5 5.3 pad_maximum_fusion
  628.8 5.7 reshape.88
  634.5 8.1 %gather_fusion.1 = bf16[1024,896]{1,0:T(8,128)(2,1)} fusion(bf16[1920,896]{1,0:T(8,128)(2,1)} %reshape.88, s32[1024]{0:T(1024)S(1)} %broadcast_clamp_fusion), kind=kCustom, calls=%fused_computation.1 | custom fusion | bytes 3674112 | tf_op jit(solution)/shard_map/gather | solution.py:61
  642.6 3.4 fusion
  (51 shorter events, 25.5 us)
Async XLA Ops:
  6.5 242.0 %copy-start = (bf16[1,896,1024]{2,1,0:T(8,128)(2,1)S(1)}, bf16[1,896,1024]{2,1,0:T(8,128)(2,1)}, u32[]{:S(2)}) copy-start(bf16[1,896,1024]{2,1,0:T(8,128)(2,1)} %param.8) | copy-start | bytes 5505028
  7.5 6.3 copy-start.1
  236.7 96.7 %all-to-all-start.4 = ((bf16[128,5,896]{2,1,0:T(8,128)(2,1)}), bf16[128,5,896]{2,1,0:T(8,128)(2,1)}, u32[]{:S(2)}, u32[]{:S(2)}) async-start(bf16[128,5,896]{2,1,0:T(8,128)(2,1)} %get-tuple-element.10), calls=%async_computation.4 | async-start | bytes 3670016 | tf_op jit(solution)/shard_map/all_to_all | solution.py:19
  245.8 68.7 %all-reduce.5.cloned.1.call-start = ((), (), s32[]{:S(2)}) async-start(), calls=%async_computation.6 | async-start | bytes 2621440 | tf_op jit(solution)/shard_map/psum | solution.py:12
  314.6 2.2 copy-start.3
  333.4 96.7 %all-to-all-start.1 = ((bf16[128,5,896]{2,1,0:T(8,128)(2,1)}), bf16[128,5,896]{2,1,0:T(8,128)(2,1)}, u32[]{:S(2)}, u32[]{:S(2)}) async-start(bf16[128,5,896]{2,1,0:T(8,128)(2,1)} %reshape.83), calls=%async_computation.1 | async-start | bytes 3670016 | tf_op jit(solution)/shard_map/all_to_all | solution.py:27
  342.5 68.6 %all-reduce.7.cloned.1.call-start = ((), (), s32[]{:S(2)}) async-start(), calls=%async_computation.7 | async-start | bytes 2621440 | tf_op jit(solution)/shard_map/psum | solution.py:12
  411.1 2.2 copy-start.4
  430.1 96.7 %all-to-all-start.3 = ((bf16[128,5,896]{2,1,0:T(8,128)(2,1)}), bf16[128,5,896]{2,1,0:T(8,128)(2,1)}, u32[]{:S(2)}, u32[]{:S(2)}) async-start(bf16[128,5,896]{2,1,0:T(8,128)(2,1)} %reshape.85), calls=%async_computation.3 | async-start | bytes 3670016 | tf_op jit(solution)/shard_map/all_to_all | solution.py:27
  439.2 68.8 %all-reduce.9.cloned.1.call-start = ((), (), s32[]{:S(2)}) async-start(), calls=%async_computation.8 | async-start | bytes 2621440 | tf_op jit(solution)/shard_map/psum | solution.py:12
  513.0 23.0 %copy-start.2 = (f32[128,8]{0,1:T(8,128)S(1)}, f32[128,8]{0,1:T(8,128)}, u32[]{:S(2)}) copy-start(f32[128,8]{0,1:T(8,128)} %param.7) | copy-start | bytes 12292
  526.8 96.7 %all-to-all-start.5 = ((bf16[128,5,896]{2,1,0:T(8,128)(2,1)}), bf16[128,5,896]{2,1,0:T(8,128)(2,1)}, u32[]{:S(2)}, u32[]{:S(2)}) async-start(bf16[128,5,896]{2,1,0:T(8,128)(2,1)} %reshape.87), calls=%async_computation.5 | async-start | bytes 3670016 | tf_op jit(solution)/shard_map/all_to_all | solution.py:27
Sparse Core Ops, SparseCore 0:
  251.3 63.2 all-reduce.4
  347.8 63.2 all-reduce.6
  444.7 63.2 all-reduce.8
where the time goes:
time: 654 us; the launch traced here: 653 us
  waiting for transfers between devices  319 us (49%)
  blocking collectives  205 us (31%)
  local copies, waits for them, and re-layouts  50 us (8%)
  starting transfers between devices  37 us (6%)
  other arithmetic  14.5 us (2%)
  matrix products  14.3 us (2%)
  between operations  13.4 us (2%)
    all_to_all x2, blocking collectives, expert_chunk(): lax.all_to_all(piece, 'expert', split_axis=0, concat_axis=0, tiled=True)  205 us
    psum x3, waiting for transfers between devices, silu_hidden(): summed = lax.psum(before.astype(jnp.bfloat16), 'dp').astype(jnp.float32)  190 us
    all_to_all x3, waiting for transfers between devices, expert_chunk(): lax.all_to_all(outcome, 'expert', split_axis=0, concat_axis=0, tiled=True)  115 us
    all_to_all x3, starting transfers between devices, expert_chunk(): lax.all_to_all(outcome, 'expert', split_axis=0, concat_axis=0, tiled=True)  27.4 us
    all_to_all x1, waiting for transfers between devices, expert_chunk(): lax.all_to_all(piece, 'expert', split_axis=0, concat_axis=0, tiled=True)  13.6 us
  transfers between devices with their start and end apart: 7, of which 7 were waited for; matrix products, arithmetic and copies ran while one was open for 5% of the time, Pallas kernels for 0%

commit v1 on v0

--- a/solution.py
+++ b/solution.py
@@ -9,7 +9,7 @@
 
 
 def silu_hidden(before):
-    summed = lax.psum(before.astype(jnp.bfloat16), "dp").astype(jnp.float32)
+    summed = jnp.sum(lax.all_gather(before.astype(jnp.bfloat16), "dp"), axis=0).astype(jnp.float32)
     result = jax.nn.silu(summed).astype(jnp.bfloat16)
     return result
 

time: 654 us -> 682 us (1.043)
  blocking collectives: 205 us -> 302 us
  waiting for transfers between devices: 319 us -> 239 us
  other arithmetic: 14.5 us -> 24.8 us
  starting transfers between devices: 37 us -> 27.4 us
    psum x3 -> x0, waiting for transfers between devices: 190 us -> none  [silu_hidden(): summed = lax.psum(before.astype(jnp.bfloat16), 'dp').astype(jnp.float32)]
    all_to_all x3, waiting for transfers between devices: 115 us -> 239 us  [expert_chunk(): lax.all_to_all(outcome, 'expert', split_axis=0, concat_axis=0, tiled=True)]
    all_to_all x2 -> x3, blocking collectives: 205 us -> 302 us  [expert_chunk(): lax.all_to_all(piece, 'expert', split_axis=0, concat_axis=0, tiled=True)]
    all_to_all x1 -> x0, waiting for transfers between devices: 13.6 us -> none  [expert_chunk(): lax.all_to_all(piece, 'expert', split_axis=0, concat_axis=0, tiled=True)]
    reduce_sum x0 -> x3, other arithmetic: none -> 12.3 us  [silu_hidden(): jnp.sum(lax.all_gather(before.astype(jnp.bfloat16), 'dp'), axis=0)]
    all_to_all x1 -> x0, starting transfers between devices: 9.13 us -> none  [expert_chunk(): lax.all_to_all(piece, 'expert', split_axis=0, concat_axis=0, tiled=True)]
  transfers between devices with their start and end apart: 7 -> 6, of which waited for: 7 -> 3; matrix products, arithmetic and copies ran while one was open for 5% -> 6% of each run, Pallas kernels for 0% -> 0%
where the time goes in v1:
time: 682 us; the launch traced here: 680 us
  blocking collectives  302 us (44%)
  waiting for transfers between devices  239 us (35%)
  local copies, waits for them, and re-layouts  55.3 us (8%)
  starting transfers between devices  27.4 us (4%)
  other arithmetic  24.8 us (4%)
  matrix products  18.9 us (3%)
  between operations  13.3 us (2%)
    all_to_all x3, blocking collectives, expert_chunk(): lax.all_to_all(piece, 'expert', split_axis=0, concat_axis=0, tiled=True)  302 us
    all_to_all x3, waiting for transfers between devices, expert_chunk(): lax.all_to_all(outcome, 'expert', split_axis=0, concat_axis=0, tiled=True)  239 us
    all_to_all x3, starting transfers between devices, expert_chunk(): lax.all_to_all(outcome, 'expert', split_axis=0, concat_axis=0, tiled=True)  27.1 us
  transfers between devices with their start and end apart: 6, of which 3 were waited for; matrix products, arithmetic and copies ran while one was open for 6% of the time, Pallas kernels for 0%

profile of v1, /device:TPU:1, one launch (start us, length us, event | category | flops | bytes accessed | tf_op | source)
XLA Modules:
  0.0 680.3 jit_solution(17452881831499892103)
XLA Ops:
  9.4 4.3 scatter_custom_fusion
  13.8 7.1 %gather_fusion = bf16[1920,896]{1,0:T(8,128)(2,1)} fusion(bf16[129,896]{1,0:T(8,128)(2,1)S(1)} %concatenate.6, s32[2048]{0:T(1024)S(1)} %pad_clamp_fusion), kind=kCustom, calls=%fused_computation | custom fusion | bytes 6888960 | tf_op jit(solution)/shard_map/gather | solution.py:53
  21.0 5.7 reshape.81
  26.7 6.0 fusion.48
  32.7 108.1 %all_to_all.30 = bf16[128,5,896]{2,1,0:T(8,128)(2,1)} all-to-all(bf16[128,5,896]{2,1,0:T(8,128)(2,1)S(1)} %get-tuple-element.9), channel_id=1, replica_groups=mesh['expert'=128,'dp'=4] {'expert'}, dimensions={0} | all-to-all | bytes 2293760 | tf_op jit(solution)/shard_map/all_to_all | solution.py:19
  146.0 96.7 %all_to_all.31 = bf16[128,5,896]{2,1,0:T(8,128)(2,1)} all-to-all(bf16[128,5,896]{2,1,0:T(8,128)(2,1)} %get-tuple-element.11), channel_id=1, replica_groups=mesh['expert'=128,'dp'=4] {'expert'}, dimensions={0} | all-to-all | bytes 2293760 | tf_op jit(solution)/shard_map/all_to_all | solution.py:19
  247.8 4.1 reduce_sum.68
  253.7 96.7 %all_to_all.32 = bf16[128,5,896]{2,1,0:T(8,128)(2,1)} all-to-all(bf16[128,5,896]{2,1,0:T(8,128)(2,1)} %get-tuple-element.10), channel_id=1, replica_groups=mesh['expert'=128,'dp'=4] {'expert'}, dimensions={0} | all-to-all | bytes 2293760 | tf_op jit(solution)/shard_map/all_to_all | solution.py:19
  350.4 3.6 reshape.86
  354.0 4.0 fusion.28
  358.0 3.3 reshape.83
  361.3 9.3 %all-to-all-start.1 = ((bf16[128,5,896]{2,1,0:T(8,128)(2,1)}), bf16[128,5,896]{2,1,0:T(8,128)(2,1)}, u32[]{:S(2)}, u32[]{:S(2)}) async-start(bf16[128,5,896]{2,1,0:T(8,128)(2,1)} %reshape.83), calls=%async_computation.1 | async-start | bytes 3670016 | tf_op jit(solution)/shard_map/all_to_all | solution.py:27
  373.4 4.1 reduce_sum.69
  382.9 75.3 %all-to-all-done.1 = bf16[128,5,896]{2,1,0:T(8,128)(2,1)} async-done(((bf16[128,5,896]{2,1,0:T(8,128)(2,1)}), bf16[128,5,896]{2,1,0:T(8,128)(2,1)}, u32[]{:S(2)}, u32[]{:S(2)}) %all-to-all-start.1) | async-done | bytes 1146912 | tf_op jit(solution)/shard_map/all_to_all | solution.py:27
  458.1 8.7 %all-to-all-start.3 = ((bf16[128,5,896]{2,1,0:T(8,128)(2,1)}), bf16[128,5,896]{2,1,0:T(8,128)(2,1)S(1)}, u32[]{:S(2)}, u32[]{:S(2)}) async-start(bf16[128,5,896]{2,1,0:T(8,128)(2,1)} %reshape.85), calls=%async_computation.3 | async-start | bytes 3670016 | tf_op jit(solution)/shard_map/all_to_all | solution.py:27
  466.9 4.1 reduce_sum.70
  471.0 4.0 fusion.34
  478.3 76.4 %all-to-all-done.3 = bf16[128,5,896]{2,1,0:T(8,128)(2,1)S(1)} async-done(((bf16[128,5,896]{2,1,0:T(8,128)(2,1)}), bf16[128,5,896]{2,1,0:T(8,128)(2,1)S(1)}, u32[]{:S(2)}, u32[]{:S(2)}) %all-to-all-start.3) | async-done | bytes 1146912 | tf_op jit(solution)/shard_map/all_to_all | solution.py:27
  554.7 9.1 %all-to-all-start.5 = ((bf16[128,5,896]{2,1,0:T(8,128)(2,1)}), bf16[128,5,896]{2,1,0:T(8,128)(2,1)}, u32[]{:S(2)}, u32[]{:S(2)}) async-start(bf16[128,5,896]{2,1,0:T(8,128)(2,1)} %reshape.87), calls=%async_computation.5 | async-start | bytes 3670016 | tf_op jit(solution)/shard_map/all_to_all | solution.py:27
  564.0 87.4 %all-to-all-done.5 = bf16[128,5,896]{2,1,0:T(8,128)(2,1)} async-done(((bf16[128,5,896]{2,1,0:T(8,128)(2,1)}), bf16[128,5,896]{2,1,0:T(8,128)(2,1)}, u32[]{:S(2)}, u32[]{:S(2)}) %all-to-all-start.5) | async-done | bytes 1146912 | tf_op jit(solution)/shard_map/all_to_all | solution.py:27
  651.4 5.0 pad_maximum_fusion
  656.4 5.7 reshape.88
  662.1 8.3 %gather_fusion.1 = bf16[1024,896]{1,0:T(8,128)(2,1)} fusion(bf16[1920,896]{1,0:T(8,128)(2,1)} %reshape.88, s32[1024]{0:T(1024)S(1)} %broadcast_clamp_fusion), kind=kCustom, calls=%fused_computation.1 | custom fusion | bytes 3674112 | tf_op jit(solution)/shard_map/gather | solution.py:61
  670.4 3.4 fusion
  (55 shorter events, 26.5 us)
Async XLA Ops:
  6.5 136.8 %copy-start = (bf16[1,896,1024]{2,1,0:T(8,128)(2,1)S(1)}, bf16[1,896,1024]{2,1,0:T(8,128)(2,1)}, u32[]{:S(2)}) copy-start(bf16[1,896,1024]{2,1,0:T(8,128)(2,1)} %param.8) | copy-start | bytes 5505028
  6.5 241.2 %all-gather.7.cloned.1.call-start = ((), (), s32[]{:S(2)}) async-start(), calls=%async_computation.6 | async-start | bytes 6553600 | tf_op jit(solution)/shard_map/all_gather | solution.py:12
  8.1 5.7 copy-start.4
  145.9 227.5 %all-gather.9.cloned.1.call-start = ((), (), s32[]{:S(2)}) async-start(), calls=%async_computation.7 | async-start | bytes 6553600 | tf_op jit(solution)/shard_map/all_gather | solution.py:12
  350.4 3.6 copy-start.2
  361.3 9.5 %copy-start.3 = (bf16[640,896]{1,0:T(8,128)(2,1)S(1)}, bf16[640,896]{1,0:T(8,128)(2,1)}, u32[]{:S(2)}) copy-start(bf16[640,896]{1,0:T(8,128)(2,1)} %reshape.86) | copy-start | bytes 3440644
  361.3 96.8 %all-to-all-start.1 = ((bf16[128,5,896]{2,1,0:T(8,128)(2,1)}), bf16[128,5,896]{2,1,0:T(8,128)(2,1)}, u32[]{:S(2)}, u32[]{:S(2)}) async-start(bf16[128,5,896]{2,1,0:T(8,128)(2,1)} %reshape.83), calls=%async_computation.1 | async-start | bytes 3670016 | tf_op jit(solution)/shard_map/all_to_all | solution.py:27
  370.6 96.3 %all-gather.11.cloned.1.call-start = ((), (), s32[]{:S(2)}) async-start(), calls=%async_computation.8 | async-start | bytes 6553600 | tf_op jit(solution)/shard_map/all_gather | solution.py:12
  458.1 96.6 %all-to-all-start.3 = ((bf16[128,5,896]{2,1,0:T(8,128)(2,1)}), bf16[128,5,896]{2,1,0:T(8,128)(2,1)S(1)}, u32[]{:S(2)}, u32[]{:S(2)}) async-start(bf16[128,5,896]{2,1,0:T(8,128)(2,1)} %reshape.85), calls=%async_computation.3 | async-start | bytes 3670016 | tf_op jit(solution)/shard_map/all_to_all | solution.py:27
  478.3 85.5 %copy-start.5 = (f32[128,8]{0,1:T(8,128)S(1)}, f32[128,8]{0,1:T(8,128)}, u32[]{:S(2)}) copy-start(f32[128,8]{0,1:T(8,128)} %param.7) | copy-start | bytes 12292
  554.7 96.7 %all-to-all-start.5 = ((bf16[128,5,896]{2,1,0:T(8,128)(2,1)}), bf16[128,5,896]{2,1,0:T(8,128)(2,1)}, u32[]{:S(2)}, u32[]{:S(2)}) async-start(bf16[128,5,896]{2,1,0:T(8,128)(2,1)} %reshape.87), calls=%async_computation.5 | async-start | bytes 3670016 | tf_op jit(solution)/shard_map/all_to_all | solution.py:27
  662.1 11.7 %copy-start.1 = (bf16[1,896,1024]{2,1,0:T(8,128)(2,1)S(1)}, bf16[1,896,1024]{2,1,0:T(8,128)(2,1)}, u32[]{:S(2)}) copy-start(bf16[1,896,1024]{2,1,0:T(8,128)(2,1)} %param.8) | copy-start | bytes 5505028
Sparse Core Ops, SparseCore 0:
  146.0 58.0 all-gather.6
  253.8 58.0 all-gather.8
  378.5 65.5 all-gather.10
